TPU v7x, 32 devices: a whole 2x2x4 slice. The times are simulated.
32 devices in a mesh: ang: 8 (over z, core), row: 4 (over y, x).
Axes of the slice: x: 2, y: 2, z: 4, core: 2. Of those that a mesh axis runs over, the one named last changes fastest.
Arguments:
- panels: bfloat16 [4, 32, 64, 2, 128], P('row', None, 'ang'), may hold values from -6 to 6
- panel_slot: int32 [4, 32], P('row'), may hold values from 0 to 15
- panel_cell: int32 [4, 32, 2], P('row'), may hold values from 0 to 15
- bloch_k: float32 [8, 2], replicated, may hold values from -3.140625 to 3.140625
- leaf_inverse: bfloat16 [8, 2, 8192, 256], P('ang', None, 'row'), may hold values from -0.25 to 0.25
- level_left: bfloat16 [8, 3, 2, 32, 8192], P('ang', None, None, None, 'row'), may hold values from -0.75 to 0.75
- level_right: bfloat16 [8, 3, 2, 32, 8192], P('ang', None, None, None, 'row'), may hold values from -0.125 to 0.125
- block_left: bfloat16 [8, 2, 32, 8192], P('ang', None, None, 'row'), may hold values from -0.75 to 0.75
- block_right: bfloat16 [8, 2, 32, 8192], P('ang', None, None, 'row'), may hold values from -0.09375 to 0.09375
- block_coupling: bfloat16 [8, 4, 2, 32, 128], P('ang', 'row'), may hold values from -0.375 to 0.375
- rank_count: int32 [8, 4], P('ang', 'row'), may hold values from 16 to 32
- quad_weight: float32 [8, 2], P('ang'), may hold values from -2 to 2
Outputs:
- response: float32 [64, 2, 8192], P('ang', None, 'row')
All inputs are finite; a program needn't handle non-finite values.
Results may differ from a plain program's by a relative error of at most 0.0045.
Values may be sent and summed in bfloat16 or wider, within the bound.
No kernel may reach another device: no remote copies, remote signals or barrier semaphores. Data moves between devices by JAX's collectives and lax.ppermute only.
A program may use at most 64 MiB of HBM per device.

v0:
```python
import jax
import jax.numpy as jnp
from jax import lax
from jax.sharding import PartitionSpec as P


def complex_product(form, left_real, left_imag, right_real, right_imag):

    def single(first, second):
        return jnp.einsum(form, first, second, preferred_element_type=jnp.float32)

    return (
        single(left_real, right_real) - single(left_imag, right_imag),
        single(left_real, right_imag) + single(left_imag, right_real),
    )


def assemble(phase_cosine, phase_sin, onehot, panel_group):
    coef_cos = phase_cosine[:, :, None] * onehot[None]
    coef_sin = phase_sin[:, :, None] * onehot[None]
    panel_real = panel_group[:, :, 0]
    panel_imag = panel_group[:, :, 1]

    def single(coefficient, entry_values):
        return jnp.einsum(
            "aqk,qsw->askw", coefficient, entry_values, preferred_element_type=jnp.float32
        )

    real_part = single(coef_cos, panel_real) + single(coef_sin, panel_imag)
    imag_part = single(coef_cos, panel_imag) - single(coef_sin, panel_real)
    stacked = jnp.stack([real_part, imag_part], 2)
    dims = stacked.shape
    return stacked.reshape(dims[0], dims[1], 2, dims[3] * dims[4]).astype(jnp.bfloat16)


def near_field(excite, leaf_block, right_factors, left_factors):
    source_count = excite.shape[0]
    row_count = excite.shape[2]
    leaf_width = leaf_block.shape[2]
    leaf_count = row_count // leaf_width
    rank_width = right_factors.shape[2]
    gathered_groups = excite.reshape(source_count, 2, leaf_count, leaf_width)
    real_part, imag_part = complex_product(
        "lwv,slv->slw",
        leaf_block[0].reshape(leaf_count, leaf_width, leaf_width),
        leaf_block[1].reshape(leaf_count, leaf_width, leaf_width),
        gathered_groups[:, 0],
        gathered_groups[:, 1],
    )
    real_part = real_part.reshape(source_count, row_count)
    imag_part = imag_part.reshape(source_count, row_count)
    for tree_level_index in range(right_factors.shape[0]):
        node_size = row_count // 2 ** (tree_level_index + 1)
        groups = row_count // node_size
        node_view = excite.reshape(source_count, 2, groups, node_size)
        right_real = right_factors[tree_level_index, 0].reshape(rank_width, groups, node_size)
        right_imag = right_factors[tree_level_index, 1].reshape(rank_width, groups, node_size)
        proj_real, proj_imag = complex_product(
            "rgm,sgm->sgr", right_real, right_imag, node_view[:, 0], node_view[:, 1]
        )
        projected = jnp.stack([proj_real, proj_imag], 1).astype(jnp.bfloat16)
        swapped = projected.reshape(source_count, 2, groups // 2, 2, rank_width)[
            :, :, :, ::-1
        ].reshape(source_count, 2, groups, rank_width)
        left_real = left_factors[tree_level_index, 0].reshape(rank_width, groups, node_size)
        left_imag = left_factors[tree_level_index, 1].reshape(rank_width, groups, node_size)
        add_real, add_imag = complex_product(
            "rgm,sgr->sgm", left_real, left_imag, swapped[:, 0], swapped[:, 1]
        )
        real_part = real_part + add_real.reshape(source_count, row_count)
        imag_part = imag_part + add_imag.reshape(source_count, row_count)
    return (real_part, imag_part)


def shards(
    panels,
    panel_slot,
    panel_cell,
    bloch_k,
    leaf_inverse,
    level_left,
    level_right,
    block_left,
    block_right,
    block_coupling,
    rank_count,
    quad_weight,
):
    local_angles = leaf_inverse.shape[0]
    row_count = leaf_inverse.shape[2]
    panel_width = panels.shape[4]
    slot_count = row_count // panel_width
    onehot = (panel_slot[0][:, None] == jnp.arange(slot_count, dtype=jnp.int32)[None, :]).astype(
        jnp.bfloat16
    )
    cell_float = panel_cell[0].astype(jnp.float32)
    own_wave = lax.dynamic_slice_in_dim(
        bloch_k, lax.axis_index("ang") * local_angles, local_angles, 0
    )
    theta = own_wave[:, 0:1] * cell_float[None, :, 0] + own_wave[:, 1:2] * cell_float[None, :, 1]
    own_cos = jnp.cos(theta).astype(jnp.bfloat16)
    own_sin = jnp.sin(theta).astype(jnp.bfloat16)
    excitation = assemble(
        own_cos, own_sin, onehot, lax.all_gather(panels, "ang", axis=2, tiled=True)[0]
    )
    rank_width = block_right.shape[2]
    rank_iota = jnp.arange(rank_width, dtype=jnp.int32)
    rank_masks = (rank_iota[None, :] < rank_count).astype(jnp.bfloat16)
    right_masked = block_right * rank_masks[:, None, :, None]
    left_masked = block_left * rank_masks[:, None, :, None]
    proj_real, proj_imag = complex_product(
        "arm,asm->asr",
        right_masked[:, 0],
        right_masked[:, 1],
        excitation[:, :, 0],
        excitation[:, :, 1],
    )
    projected = jnp.stack([proj_real, proj_imag], 2).astype(jnp.bfloat16)
    gathered = lax.all_gather(projected[:, None], "row", axis=1, tiled=True)
    number_of_blocks = gathered.shape[1]
    keep_other = (jnp.arange(number_of_blocks, dtype=jnp.int32) != lax.axis_index("row")).astype(
        jnp.bfloat16
    )
    gathered = gathered * keep_other[None, :, None, None, None]
    coupling = block_coupling[:, 0].reshape(
        local_angles, 2, rank_width, number_of_blocks, rank_width
    )
    coup_real, coup_imag = complex_product(
        "arjq,ajsq->asr", coupling[:, 0], coupling[:, 1], gathered[:, :, :, 0], gathered[:, :, :, 1]
    )
    coupled = jnp.stack([coup_real, coup_imag], 2).astype(jnp.bfloat16)
    excite_part = excitation[0]
    coupled_part = coupled[0]
    near_real, near_imag = near_field(excite_part, leaf_inverse[0], level_right[0], level_left[0])
    far_real, far_imag = complex_product(
        "rm,sr->sm", left_masked[0, 0], left_masked[0, 1], coupled_part[:, 0], coupled_part[:, 1]
    )
    field_real = near_real + far_real
    field_imag = near_imag + far_imag
    weight_real = quad_weight[0, 0]
    weight_imag = quad_weight[0, 1]
    summed = jnp.stack(
        [
            weight_real * field_real - weight_imag * field_imag,
            weight_real * field_imag + weight_imag * field_real,
        ],
        1,
    )
    return lax.psum_scatter(summed, "ang", scatter_dimension=0, tiled=True)


def solution(mesh):
    placed = (
        P("row", None, "ang", None, None),
        P("row", None),
        P("row", None, None),
        P(),
        P("ang", None, "row", None),
        P("ang", None, None, None, "row"),
        P("ang", None, None, None, "row"),
        P("ang", None, None, "row"),
        P("ang", None, None, "row"),
        P("ang", "row", None, None, None),
        P("ang", "row"),
        P("ang", None),
    )
    return jax.shard_map(
        shards, mesh=mesh, in_specs=placed, out_specs=P("ang", None, "row"), check_vma=False
    )
```

profile of v0, /device:TPU:0, one launch (start us, length us, event | category | flops | bytes accessed | tf_op | source)
XLA Modules:
  0.0 121.3 jit_solution(7901270127954322322)
XLA Ops:
  6.5 1.7 %copy.87 = bf16[1,32,8,2,128]{4,1,2,3,0:T(8,128)(2,1)} copy(bf16[1,32,8,2,128]{4,3,2,1,0:T(2,128)(2,1)} %param.12) | data formatting | bytes 262144 | tf_op args[0]
  9.0 1.3 %fusion.122 = (bf16[1,1,32,2048]{3,2,1,0:T(8,128)(2,1)S(1)}, bf16[1,1,32,2048]{3,2,1,0:T(8,128)(2,1)S(1)}, bf16[1,1,32,2048]{3,2,1,0:T(8,128)(2,1)S(1)}, bf16[1,...) fusion(bf16[3,2,32,2048]{3,2,1,0:T(8,128)(2,1)} %bitcast.282), kind=kLoop, calls=%fused_computation.173 | loop fusion | bytes 1572864 | tf_op jit(solution)/shard_map/slice | solution.py:57
  20.3 1.3 %convert_bitcast_fusion.1 = (bf16[32]{0:T(256)(128)(2,1)S(1)}, f32[32,1]{0,1:T(1,128)S(1)}) fusion(f32[32,2]{0,1:T(2,128)S(1)} %convert_bitcast_fusion, f32[]{:T(128)} %bitcast.4, f32[]{:T(128)} %bitcast.2), kind=kLoop, calls=%fused_computation.163 | loop fusion | flops 128 | bytes 456 | tf_op jit(solution)/shard_map/convert_element_type | solution.py:102
  22.3 0.9 broadcast_multiply_fusion
  23.2 1.7 %fusion.120 = (bf16[1,1,2048,256]{3,2,1,0:T(8,128)(2,1)S(1)}, bf16[1,1,2048,256]{3,2,1,0:T(8,128)(2,1)S(1)}) fusion(bf16[1,2,2048,256]{3,2,1,0:T(8,128)(2,1)} %param.16), kind=kLoop, calls=%fused_computation.171 | loop fusion | bytes 4194304 | tf_op jit(solution)/shard_map/slice | solution.py:46
  24.9 8.9 %all-gather.2.cloned.1.call-done = bf16[1,32,64,2,128]{4,1,2,3,0:T(8,128)(2,1)} async-done(((bf16[1,32,8,2,128]{4,1,2,3,0:T(8,128)(2,1)}), bf16[1,32,64,2,128]{4,1,2,3,0:T(8,128)(2,1)}) %all-gather.2.cloned.1.call-update) | async-done | bytes 1048592 | tf_op jit(solution)/shard_map/all_gather | solution.py:104
  33.9 1.3 %fusion.28 = f32[16,64,128]{2,0,1:T(8,128)S(1)} fusion(bf16[32,64,2,128]{3,0,1,2:T(8,128)(2,1)} %bitcast.250, s32[32]{0:T(128)S(1)} %bitcast.298, bf16[32]{0:T(256)(128)(2,1)S(1)} %convert_bitcast_fusion.2), kind=kOutput, calls=%fused_computation.57 | convolution fusion | flops 8389632 | bytes 1048768 | tf_op jit(solution)/shard_map/aqk,qsw->askw/dot_general | solution.py:25
  35.2 2.1 %fusion.29 = f32[16,64,128]{2,0,1:T(8,128)} fusion(bf16[32,64,2,128]{3,0,1,2:T(8,128)(2,1)} %bitcast.251, s32[32]{0:T(128)S(1)} %bitcast.299, bf16[32]{0:T(256)(128)(2,1)S(1)} %convert_bitcast_fusion.2), kind=kOutput, calls=%fused_computation.58 | convolution fusion | flops 8389632 | bytes 1048768 | tf_op jit(solution)/shard_map/aqk,qsw->askw/dot_general | solution.py:25
  39.0 2.0 %fusion.11 = bf16[16,64,128]{2,0,1:T(8,128)(2,1)} fusion(f32[16,64,128]{2,0,1:T(8,128)} %fusion.29, bf16[32,64,2,128]{3,0,1,2:T(8,128)(2,1)S(1)} %bitcast.253, s32[32]{0:T(128)S(1)} %bitcast.301, bf16[32]{0:T(256)(128)(2,1)S(1)} %get-tuple-element.5), kind=kOutput, calls=%fused_computation.23 | convolution fusion | flops 8651776 | bytes 1311744 | tf_op jit(solution)/shard_map/aqk,qsw->askw/dot_general | solution.py:25
  41.0 1.1 squeeze.95
  42.1 1.7 %squeeze.90 = bf16[64,2,1024]{2,1,0:T(2,128)(2,1)} reshape(bf16[1,64,16,128]{3,2,1,0:T(8,128)(2,1)} %bitcast.260) | data formatting | bytes 524288 | tf_op jit(solution)/shard_map/squeeze | solution.py:59
  43.9 1.2 fusion.44
  45.1 1.1 fusion.40
  46.7 1.1 fusion.78
  47.8 1.1 fusion.80
  49.1 1.1 fusion.34
  50.2 1.1 fusion.30
  51.3 1.1 fusion.27
  52.4 1.1 fusion.26
  53.6 8.2 %all_gather.7 = bf16[1,4,64,2,32]{2,4,3,0,1:T(8,128)(2,1)S(1)} all-gather(bf16[1,1,64,2,32]{2,4,3,0,1:T(8,128)(2,1)S(1)} %maximum_bitcast_fusion), channel_id=1, replica_groups=mesh['ang'=8,'row'=4] {'row'}, dimensions={1}, use_global_device_ids=true | all-gather | bytes 40960 | tf_op jit(solution)/shard_map/all_gather | solution.py:119
  61.8 1.5 %convolution_bitcast_fusion = f32[64,32]{0,1:T(8,128)} fusion(bf16[1,1,32,4,32]{4,3,2,1,0:T(4,128)(2,1)} %get-tuple-element.24, bf16[1,4,64,2,32]{2,4,1,3,0:T(8,128)(2,1)S(1)} %copy_multiply_fusion), kind=kOutput, calls=%fused_computation.36 | convolution fusion | flops 524288 | bytes 49152 | tf_op jit(solution)/shard_map/arjq,ajsq->asr/dot_general | solution.py:10
  63.3 1.5 %convolution_bitcast_fusion.2 = f32[64,32]{0,1:T(8,128)} fusion(bf16[1,1,32,4,32]{4,3,2,1,0:T(4,128)(2,1)} %get-tuple-element.24, bf16[1,4,64,2,32]{2,4,1,3,0:T(8,128)(2,1)S(1)} %copy_multiply_fusion), kind=kOutput, calls=%fused_computation.38 | convolution fusion | flops 524288 | bytes 49152 | tf_op jit(solution)/shard_map/arjq,ajsq->asr/dot_general | solution.py:10
  64.9 1.1 fusion.60
  66.0 1.1 fusion.54
  67.6 1.1 fusion.70
  68.7 1.1 fusion.68
  69.8 1.2 %fusion.62 = f32[8,64,256]{2,1,0:T(8,128)} fusion(bf16[8,256,256]{2,1,0:T(8,128)(2,1)S(1)} %bitcast.246, bf16[64,8,256]{2,1,0:T(8,128)(2,1)S(1)} %squeeze.86), kind=kOutput, calls=%fused_computation.91 | convolution fusion | flops 67108864 | bytes 1835008 | tf_op jit(solution)/shard_map/lwv,slv->slw/dot_general | solution.py:10
  71.0 1.2 %fusion.52 = f32[8,64,256]{2,1,0:T(8,128)} fusion(bf16[8,256,256]{2,1,0:T(8,128)(2,1)S(1)} %bitcast.247, bf16[64,8,256]{2,1,0:T(8,128)(2,1)S(1)} %squeeze.87), kind=kOutput, calls=%fused_computation.81 | convolution fusion | flops 67108864 | bytes 1835008 | tf_op jit(solution)/shard_map/lwv,slv->slw/dot_general | solution.py:10
  78.9 1.7 %subtract_bitcast_fusion = (f32[64,1,2048]{2,0,1:T(8,128)S(1)}, f32[64,1,2048]{2,0,1:T(8,128)S(1)}) fusion(f32[64,2048]{1,0:T(8,128)S(1)} %fusion, f32[]{:T(128)} %bitcast.66, f32[]{:T(128)} %bitcast, f32[64,2048]{1,0:T(8,128)S(1)} %fusion.64, bf16[64,32]{0,1:T(8,128)(2,1)S(1)} %fusion.23, bf16[1,2,32,2048]{3,2,1,0:T(8,128)(2,1)S(1)} %copy-done.3, ...), kind=kOutput, calls=%fused_computation.56 | convolution fusion | flops 9830400 | bytes 4333576 | tf_op jit(solution)/shard_map/rm,sr->sm/dot_general | solution.py:10
  80.6 1.1 pad_maximum_fusion
  81.7 31.1 %reduce-scatter.2.cloned.1.call-done = f32[8,2,2048]{2,0,1:T(8,128)} async-done(((f32[64,2,2048]{2,0,1:T(8,128)}), f32[8,2,2048]{2,0,1:T(8,128)}) %reduce-scatter.2.cloned.1.call-update) | async-done | bytes 131088 | tf_op jit(solution)/shard_map/reduce_scatter | solution.py:149
  112.8 1.7 %copy.140 = f32[8,2,2048]{2,1,0:T(2,128)} copy(f32[8,2,2048]{2,0,1:T(8,128)} %reduce-scatter.2.cloned.1.call-done) | data formatting | bytes 262144 | tf_op jit(solution)/shard_map/reduce_scatter | solution.py:149
  (152 shorter events, 20.1 us)
Async XLA Ops:
  6.5 5.2 %copy-start = (f32[8,2]{0,1:T(2,128)S(1)}, f32[8,2]{0,1:T(2,128)}, u32[]{:S(2)}) copy-start(f32[8,2]{0,1:T(2,128)} %param.15) | copy-start | bytes 196
  6.5 3.7 %copy-start.18 = (bf16[1,3,2,32,2048]{4,3,2,1,0:T(8,128)(2,1)S(1)}, bf16[1,3,2,32,2048]{4,3,2,1,0:T(8,128)(2,1)}, u32[]{:S(2)}) copy-start(bf16[1,3,2,32,2048]{4,3,2,1,0:T(8,128)(2,1)} %param.17) | copy-start | bytes 2359300
  6.5 4.5 %copy-start.40 = (f32[1,2]{1,0:T(1,128)S(1)}, f32[1,2]{1,0:T(1,128)}, u32[]{:S(2)}) copy-start(f32[1,2]{1,0:T(1,128)} %param.23) | copy-start | bytes 28
  6.5 27.3 %all-gather.2.cloned.1.call-start = ((), (), s32[]{:S(2)}) async-start(), calls=%async_computation.1 | async-start | bytes 1179648 | tf_op jit(solution)/shard_map/all_gather | solution.py:104
  8.2 104.6 %reduce-scatter.2.cloned.1.call-start = ((), (), s32[]{:S(2)}) async-start(), calls=%async_computation.2 | async-start | bytes 1179648 | tf_op jit(solution)/shard_map/reduce_scatter | solution.py:149
  10.2 9.4 %copy-start.38 = (bf16[1,1,2,32,128]{4,3,2,1,0:T(8,128)(2,1)S(1)}, bf16[1,1,2,32,128]{4,3,2,1,0:T(8,128)(2,1)}, u32[]{:S(2)}) copy-start(bf16[1,1,2,32,128]{4,3,2,1,0:T(8,128)(2,1)} %param.21) | copy-start | bytes 49156
  10.3 12.0 %copy-start.29 = (bf16[1,2,32,2048]{3,2,1,0:T(8,128)(2,1)S(1)}, bf16[1,2,32,2048]{3,2,1,0:T(8,128)(2,1)}, u32[]{:S(2)}) copy-start(bf16[1,2,32,2048]{3,2,1,0:T(8,128)(2,1)} %param.19) | copy-start | bytes 786436
  10.3 12.0 %copy-start.30 = (bf16[1,2,32,2048]{3,2,1,0:T(8,128)(2,1)S(1)}, bf16[1,2,32,2048]{3,2,1,0:T(8,128)(2,1)}, u32[]{:S(2)}) copy-start(bf16[1,2,32,2048]{3,2,1,0:T(8,128)(2,1)} %param.20) | copy-start | bytes 786436
  23.2 10.6 %copy-start.39 = (s32[1,32]{1,0:T(1,128)S(1)}, s32[1,32]{1,0:T(1,128)}, u32[]{:S(2)}) copy-start(s32[1,32]{1,0:T(1,128)} %param.13) | copy-start | bytes 388
  33.8 3.4 %copy-start.1 = (bf16[1,32,64,2,128]{4,1,2,3,0:T(8,128)(2,1)S(1)}, bf16[1,32,64,2,128]{4,1,2,3,0:T(8,128)(2,1)}, u32[]{:S(2)}) copy-start(bf16[1,32,64,2,128]{4,1,2,3,0:T(8,128)(2,1)} %all-gather.2.cloned.1.call-done) | copy-start | bytes 3145732
  41.0 5.2 %copy-start.35 = (bf16[32,4,512]{2,1,0:T(4,128)(2,1)S(1)}, bf16[32,4,512]{2,1,0:T(4,128)(2,1)}, u32[]{:S(2)}) copy-start(bf16[32,4,512]{2,1,0:T(4,128)(2,1)} %reshape_squeeze.56) | copy-start | bytes 393220
  41.0 5.4 %copy-start.28 = (bf16[64,4,512]{2,1,0:T(4,128)(2,1)S(1)}, bf16[64,4,512]{2,1,0:T(4,128)(2,1)}, u32[]{:S(2)}) copy-start(bf16[64,4,512]{2,1,0:T(4,128)(2,1)} %squeeze.94) | copy-start | bytes 786436
  41.0 5.7 %copy-start.15 = (bf16[32,4,512]{2,1,0:T(4,128)(2,1)S(1)}, bf16[32,4,512]{2,1,0:T(4,128)(2,1)}, u32[]{:S(2)}) copy-start(bf16[32,4,512]{2,1,0:T(4,128)(2,1)} %reshape_squeeze.57) | copy-start | bytes 393220
  43.9 5.1 %copy-start.2 = (bf16[16,64,128]{2,0,1:T(8,128)(2,1)S(1)}, bf16[16,64,128]{2,0,1:T(8,128)(2,1)}, u32[]{:S(2)}) copy-start(bf16[16,64,128]{2,0,1:T(8,128)(2,1)} %fusion.11) | copy-start | bytes 786436
  46.7 2.2 %copy-start.21 = (bf16[64,2,2,2,32]{0,4,3,2,1:T(8,128)(2,1)}, bf16[64,2,2,2,32]{0,4,3,2,1:T(8,128)(2,1)S(1)}, u32[]{:S(2)}) copy-start(bf16[64,2,2,2,32]{0,4,3,2,1:T(8,128)(2,1)S(1)} %rev.7) | copy-start | bytes 98308
  48.9 18.2 %copy-start.14 = (bf16[4,8,8,256]{3,2,1,0:T(8,128)(2,1)S(1)}, bf16[4,8,8,256]{3,2,1,0:T(8,128)(2,1)}, u32[]{:S(2)}) copy-start(bf16[4,8,8,256]{3,2,1,0:T(8,128)(2,1)} %copy.152) | copy-start | bytes 393220
  51.3 16.4 %copy-start.13 = (bf16[4,8,8,256]{3,2,1,0:T(8,128)(2,1)S(1)}, bf16[4,8,8,256]{3,2,1,0:T(8,128)(2,1)}, u32[]{:S(2)}) copy-start(bf16[4,8,8,256]{3,2,1,0:T(8,128)(2,1)} %copy.153) | copy-start | bytes 393220
  61.8 8.0 %copy-start.19 = (bf16[1,4,64,2,32]{2,4,1,3,0:T(8,128)(2,1)}, bf16[1,4,64,2,32]{2,4,1,3,0:T(8,128)(2,1)S(1)}, u32[]{:S(2)}) copy-start(bf16[1,4,64,2,32]{2,4,1,3,0:T(8,128)(2,1)S(1)} %copy_multiply_fusion) | copy-start | bytes 98308
  67.6 4.7 %copy-start.16 = (bf16[64,2,4,2,32]{0,4,3,2,1:T(8,128)(2,1)}, bf16[64,2,4,2,32]{0,4,3,2,1:T(8,128)(2,1)S(1)}, u32[]{:S(2)}) copy-start(bf16[64,2,4,2,32]{0,4,3,2,1:T(8,128)(2,1)S(1)} %rev.8) | copy-start | bytes 196612
  68.7 3.6 %copy-start.5 = (f32[4,64,512]{2,1,0:T(8,128)S(1)}, f32[4,64,512]{2,1,0:T(8,128)}, u32[]{:S(2)}) copy-start(f32[4,64,512]{2,1,0:T(8,128)} %fusion.78) | copy-start | bytes 1572868
  68.7 3.6 %copy-start.11 = (bf16[32,4,512]{2,1,0:T(4,128)(2,1)S(1)}, bf16[32,4,512]{2,1,0:T(4,128)(2,1)}, u32[]{:S(2)}) copy-start(bf16[32,4,512]{2,1,0:T(4,128)(2,1)} %reshape_squeeze.58) | copy-start | bytes 393220
  68.7 3.6 %copy-start.22 = (bf16[64,2,2,2,32]{0,4,3,2,1:T(8,128)(2,1)S(1)}, bf16[64,2,2,2,32]{0,4,3,2,1:T(8,128)(2,1)}, u32[]{:S(2)}) copy-start(bf16[64,2,2,2,32]{0,4,3,2,1:T(8,128)(2,1)} %copy-done.21) | copy-start | bytes 98308
  71.0 1.6 %copy-start.25 = (bf16[64,2,1024]{2,1,0:T(2,128)(2,1)S(1)}, bf16[64,2,1024]{2,1,0:T(2,128)(2,1)}, u32[]{:S(2)}) copy-start(bf16[64,2,1024]{2,1,0:T(2,128)(2,1)} %squeeze.88) | copy-start | bytes 786436
  71.0 1.6 %copy-start.34 = (bf16[32,2,1024]{2,1,0:T(2,128)(2,1)S(1)}, bf16[32,2,1024]{2,1,0:T(2,128)(2,1)}, u32[]{:S(2)}) copy-start(bf16[32,2,1024]{2,1,0:T(2,128)(2,1)} %reshape_squeeze.51) | copy-start | bytes 393220
  71.0 1.8 %copy-start.27 = (bf16[64,2,1024]{2,1,0:T(2,128)(2,1)S(1)}, bf16[64,2,1024]{2,1,0:T(2,128)(2,1)}, u32[]{:S(2)}) copy-start(bf16[64,2,1024]{2,1,0:T(2,128)(2,1)} %squeeze.90) | copy-start | bytes 786436
  72.3 1.4 %copy-start.12 = (bf16[32,2,1024]{2,1,0:T(2,128)(2,1)S(1)}, bf16[32,2,1024]{2,1,0:T(2,128)(2,1)}, u32[]{:S(2)}) copy-start(bf16[32,2,1024]{2,1,0:T(2,128)(2,1)} %reshape_squeeze.53) | copy-start | bytes 393220
  73.4 1.2 copy-start.4
  73.4 1.2 copy-start.23
  73.4 1.5 %copy-start.31 = (bf16[64,2,32]{0,2,1:T(8,128)(2,1)}, bf16[64,2,32]{0,2,1:T(8,128)(2,1)S(1)}, u32[]{:S(2)}) copy-start(bf16[64,2,32]{0,2,1:T(8,128)(2,1)S(1)} %squeeze.91) | copy-start | bytes 24580
  74.6 1.3 %copy-start.36 = (f32[64,32]{0,1:T(8,128)S(1)}, f32[64,32]{0,1:T(8,128)}, u32[]{:S(2)}) copy-start(f32[64,32]{0,1:T(8,128)} %convolution_bitcast_fusion.2) | copy-start | bytes 24580
  74.6 1.5 %copy-start.8 = (f32[8,64,256]{2,1,0:T(8,128)S(1)}, f32[8,64,256]{2,1,0:T(8,128)}, u32[]{:S(2)}) copy-start(f32[8,64,256]{2,1,0:T(8,128)} %fusion.62) | copy-start | bytes 1572868
  77.0 1.2 copy-start.6
  (11 other events, 11.4 us)
Sparse Core Ops, SparseCore 0:
  9.0 24.8 all-gather.1
  81.8 30.9 reduce-scatter.1
where the time goes:
time: 122 us; the launch traced here: 121 us
  waiting for transfers between devices  40.1 us (33%)
  matrix products  31.9 us (26%)
  local copies, waits for them, and re-layouts  22.2 us (18%)
  between operations  14.7 us (12%)
  blocking collectives  8.16 us (7%)
  other arithmetic  4.16 us (3%)
    reduce_scatter x1, waiting for transfers between devices, shards(): return lax.psum_scatter(summed, 'ang', scatter_dimension=0, tiled=True)  31.1 us
    dot_general x40, matrix products, single(): return jnp.einsum(form, first, second, preferred_element_type=jnp.float32)  26.3 us
    all_gather x1, waiting for transfers between devices, shards(): lax.all_gather(panels, 'ang', axis=2, tiled=True)[0]  8.91 us
    all_gather x1, blocking collectives, shards(): gathered = lax.all_gather(projected[:, None], 'row', axis=1, tiled=True)  8.16 us
    dot_general x4, matrix products, single(): jnp.einsum('aqk,qsw->askw', coefficient, entry_values, preferred_element_...  5.57 us
    unnamed x87, local copies, waits for them, and re-layouts  5.45 us
    squeeze x2, local copies, waits for them, and re-layouts, near_field(): node_view[:, 1]  2.85 us
  transfers between devices with their start and end apart: 2, of which 2 were waited for; matrix products, arithmetic and copies ran while one was open for 13% of the time, Pallas kernels for 0%

commit v1 on v0

--- a/solution.py
+++ b/solution.py
@@ -2,6 +2,29 @@
 import jax.numpy as jnp
 from jax import lax
 from jax.sharding import PartitionSpec as P
+
+
+def push_face_in(inp, axis_name):
+    carry = lax.axis_size(axis_name)
+    v1 = lax.axis_index(axis_name)
+    response, clean, next_value = (carry, v1, inp.shape[2])
+    block_list = [(c, (c + 1) % response) for c in range(response)]
+    history = [(c, (c - 1) % response) for c in range(response)]
+    f_next = jnp.zeros((*inp.shape[:2], response * next_value, *inp.shape[3:]), inp.dtype)
+    f_next = lax.dynamic_update_slice_in_dim(f_next, inp, clean * next_value, axis=2)
+    vec_out = after = inp
+    piece_next = response // 2
+    for idx in range(1, piece_next + 1):
+        vec_out = lax.ppermute(vec_out, axis_name=axis_name, perm=block_list)
+        f_next = lax.dynamic_update_slice_in_dim(
+            f_next, vec_out, (clean - idx) % response * next_value, axis=2
+        )
+        if idx < response - piece_next:
+            after = lax.ppermute(after, axis_name=axis_name, perm=history)
+            f_next = lax.dynamic_update_slice_in_dim(
+                f_next, after, (clean + idx) % response * next_value, axis=2
+            )
+    return f_next
 
 
 def complex_product(form, left_real, left_imag, right_real, right_imag):
@@ -100,9 +123,7 @@
     theta = own_wave[:, 0:1] * cell_float[None, :, 0] + own_wave[:, 1:2] * cell_float[None, :, 1]
     own_cos = jnp.cos(theta).astype(jnp.bfloat16)
     own_sin = jnp.sin(theta).astype(jnp.bfloat16)
-    excitation = assemble(
-        own_cos, own_sin, onehot, lax.all_gather(panels, "ang", axis=2, tiled=True)[0]
-    )
+    excitation = assemble(own_cos, own_sin, onehot, push_face_in(panels, "ang")[0])
     rank_width = block_right.shape[2]
     rank_iota = jnp.arange(rank_width, dtype=jnp.int32)
     rank_masks = (rank_iota[None, :] < rank_count).astype(jnp.bfloat16)

time: 122 us -> 150 us (1.23)
  local copies, waits for them, and re-layouts: 22.2 us -> 38.7 us
  starting transfers between devices: 0.04 us -> 11.6 us
  matrix products: 31.9 us -> 28.6 us
  other arithmetic: 4.16 us -> 6.37 us
    ppermute x0 -> x7, starting transfers between devices: none -> 11.6 us  [the longest x3 11.2 us: push_face_in(): after = lax.ppermute(after, axis_name=axis_name, perm=history)]
    ppermute x0 -> x7, waiting for transfers between devices: none -> 10.8 us  [the longest x4 10.5 us: push_face_in(): vec_out = lax.ppermute(vec_out, axis_name=axis_name, perm=block_list)]
    all_gather x1 -> x0, waiting for transfers between devices: 8.91 us -> none  [shards(): lax.all_gather(panels, 'ang', axis=2, tiled=True)[0]]
    dynamic_update_slice x0 -> x8, local copies, waits for them, and re-layouts: none -> 2.91 us  [the longest x4 0.98 us: push_face_in(): lax.dynamic_update_slice_in_dim(f_next, vec_out, (clean - idx) % response...]
    unnamed x87 -> x75, local copies, waits for them, and re-layouts: 5.45 us -> 8.13 us
    dot_general x4, matrix products: 5.57 us -> 3.39 us  [single(): jnp.einsum('aqk,qsw->askw', coefficient, entry_values, preferred_element_...]
    another operation x2, local copies, waits for them, and re-layouts: 1.45 us -> 3.27 us  [near_field(): right_factors[tree_level_index, 0].reshape(rank_width, groups, node_size)]
    another operation x2, local copies, waits for them, and re-layouts: 1.45 us -> 3.26 us  [near_field(): left_factors[tree_level_index, 0].reshape(rank_width, groups, node_size)]
  transfers between devices with their start and end apart: 2 -> 8, of which waited for: 2 -> 5; matrix products, arithmetic and copies ran while one was open for 13% -> 20% of each run, Pallas kernels for 0% -> 0%
where the time goes in v1:
time: 150 us; the launch traced here: 149 us
  waiting for transfers between devices  40.6 us (27%)
  local copies, waits for them, and re-layouts  38.7 us (26%)
  matrix products  28.6 us (19%)
  between operations  14.6 us (10%)
  starting transfers between devices  11.6 us (8%)
  blocking collectives  8.87 us (6%)
  other arithmetic  6.37 us (4%)
    reduce_scatter x1, waiting for transfers between devices, shards(): return lax.psum_scatter(summed, 'ang', scatter_dimension=0, tiled=True)  29.8 us
    dot_general x40, matrix products, single(): return jnp.einsum(form, first, second, preferred_element_type=jnp.float32)  25.3 us
    ppermute x3, starting transfers between devices, push_face_in(): after = lax.ppermute(after, axis_name=axis_name, perm=history)  11.2 us
    ppermute x4, waiting for transfers between devices, push_face_in(): vec_out = lax.ppermute(vec_out, axis_name=axis_name, perm=block_list)  10.5 us
    all_gather x1, blocking collectives, shards(): gathered = lax.all_gather(projected[:, None], 'row', axis=1, tiled=True)  8.87 us
    unnamed x75, local copies, waits for them, and re-layouts  8.13 us
    squeeze x2, local copies, waits for them, and re-layouts, near_field(): node_view[:, 1]  3.5 us
    dot_general x4, matrix products, single(): jnp.einsum('aqk,qsw->askw', coefficient, entry_values, preferred_element_...  3.39 us
  transfers between devices with their start and end apart: 8, of which 5 were waited for; matrix products, arithmetic and copies ran while one was open for 20% of the time, Pallas kernels for 0%

profile of v1, /device:TPU:0, one launch (start us, length us, event | category | flops | bytes accessed | tf_op | source)
XLA Modules:
  0.0 149.5 jit_solution(15339125981658758820)
XLA Ops:
  6.5 1.7 %copy.91 = bf16[1,32,8,2,128]{4,1,2,3,0:T(8,128)(2,1)} copy(bf16[1,32,8,2,128]{4,3,2,1,0:T(2,128)(2,1)} %param.12) | data formatting | bytes 262144 | tf_op args[0]
  8.7 4.0 %collective-permute-start.1 = (bf16[1,32,8,2,128]{4,1,2,3,0:T(8,128)(2,1)}, bf16[1,32,8,2,128]{4,1,2,3,0:T(8,128)(2,1)}, u32[]{:S(2)}, u32[]{:S(2)}) collective-permute-start(bf16[1,32,8,2,128]{4,1,2,3,0:T(8,128)(2,1)} %copy.91), channel_id=1, source_target_pairs={{0,28},{4,0},{8,4},{12,8},{16,12},{20,16},{24,20},{28,24},{1,29},{... | collective-permute-start | bytes 393224 | tf_op jit(solution)/shard_map/ppermute | solution.py:23
  14.0 1.3 convert_bitcast_fusion.2
  15.4 2.0 %fusion.122 = (bf16[1,1,32,2048]{3,2,1,0:T(8,128)(2,1)}, bf16[1,1,32,2048]{3,2,1,0:T(8,128)(2,1)S(1)}, bf16[1,1,32,2048]{3,2,1,0:T(8,128)(2,1)S(1)}, bf16[1,1,32...) fusion(bf16[3,2,32,2048]{3,2,1,0:T(8,128)(2,1)} %bitcast.289), kind=kLoop, calls=%fused_computation.181 | loop fusion | bytes 1572864 | tf_op jit(solution)/shard_map/slice | solution.py:80
  20.9 1.9 %broadcast_multiply_fusion = (bf16[1,2,32,2048]{3,2,1,0:T(8,128)(2,1)}, bf16[1,2,32,2048]{3,2,1,0:T(8,128)(2,1)}) fusion(bf16[1,2,32,2048]{3,2,1,0:T(8,128)(2,1)} %param.19, bf16[32]{0:T(256)(128)(2,1)S(1)} %compare_convert_fusion.1, bf16[1,2,32,2048]{3,2,1,0:T(8,128)(2,1)} %param.20), kind=kLoop, calls=%fused_computation.106 | loop fusion | flops 262144 | bytes 1048640 | tf_op jit(solution)/shard_map/mul | solution.py:131
  23.4 1.6 %reshape_squeeze.51 = bf16[32,2,1024]{2,1,0:T(2,128)(2,1)} reshape(bf16[1,1,32,2048]{3,2,1,0:T(8,128)(2,1)} %get-tuple-element.22) | data formatting | bytes 262144 | tf_op jit(solution)/shard_map/reshape;squeeze | solution.py:79
  25.1 1.6 %reshape_squeeze.52 = bf16[32,2,1024]{2,1,0:T(2,128)(2,1)} reshape(bf16[1,1,32,2048]{3,2,1,0:T(8,128)(2,1)} %get-tuple-element.17) | data formatting | bytes 262144 | tf_op jit(solution)/shard_map/reshape;squeeze | solution.py:80
  26.7 1.6 %reshape_squeeze.53 = bf16[32,2,1024]{2,1,0:T(2,128)(2,1)} reshape(bf16[1,1,32,2048]{3,2,1,0:T(8,128)(2,1)} %get-tuple-element.16) | data formatting | bytes 262144 | tf_op jit(solution)/shard_map/reshape;squeeze | solution.py:88
  28.3 1.6 %reshape_squeeze.54 = bf16[32,2,1024]{2,1,0:T(2,128)(2,1)} reshape(bf16[1,1,32,2048]{3,2,1,0:T(8,128)(2,1)} %get-tuple-element.11) | data formatting | bytes 262144 | tf_op jit(solution)/shard_map/reshape;squeeze | solution.py:89
  30.0 1.6 %reshape_squeeze.55 = bf16[32,4,512]{2,1,0:T(4,128)(2,1)} reshape(bf16[1,1,32,2048]{3,2,1,0:T(8,128)(2,1)} %get-tuple-element.21) | data formatting | bytes 262144 | tf_op jit(solution)/shard_map/reshape;squeeze | solution.py:79
  32.3 1.6 %reshape_squeeze.57 = bf16[32,4,512]{2,1,0:T(4,128)(2,1)} reshape(bf16[1,1,32,2048]{3,2,1,0:T(8,128)(2,1)} %get-tuple-element.15) | data formatting | bytes 262144 | tf_op jit(solution)/shard_map/reshape;squeeze | solution.py:88
  36.3 1.6 %copy.159 = bf16[4,8,8,256]{3,2,1,0:T(8,128)(2,1)} copy(bf16[4,8,8,256]{3,1,2,0:T(8,128)(2,1)} %bitcast.298) | data formatting | bytes 262144
  37.9 1.6 %copy.160 = bf16[4,8,8,256]{3,2,1,0:T(8,128)(2,1)} copy(bf16[4,8,8,256]{3,1,2,0:T(8,128)(2,1)} %bitcast.297) | data formatting | bytes 262144
  39.4 1.3 fusion.125
  40.8 3.5 %collective-permute-start.3 = (bf16[1,32,8,2,128]{4,1,2,3,0:T(8,128)(2,1)}, bf16[1,32,8,2,128]{4,1,2,3,0:T(8,128)(2,1)S(1)}, u32[]{:S(2)}, u32[]{:S(2)}) collective-permute-start(bf16[1,32,8,2,128]{4,1,2,3,0:T(8,128)(2,1)} %collective-permute-done.1), channel_id=1, source_target_pairs={{0,28},{4,0},{8,4},{12,8},{16,12},{20,16},{24,20},{28,24},{1,29},{... | collective-permute-start | bytes 393224 | tf_op jit(solution)/shard_map/ppermute | solution.py:23
  46.2 1.6 %collective-permute-done.2 = bf16[1,32,8,2,128]{4,1,2,3,0:T(8,128)(2,1)S(1)} collective-permute-done((bf16[1,32,8,2,128]{4,1,2,3,0:T(8,128)(2,1)}, bf16[1,32,8,2,128]{4,1,2,3,0:T(8,128)(2,1)S(1)}, u32[]{:S(2)}, u32[]{:S(2)}) %collective-permute-start.2) | collective-permute-done | bytes 131104 | tf_op jit(solution)/shard_map/ppermute | solution.py:18
  48.0 3.6 %collective-permute-start.5 = (bf16[1,32,8,2,128]{4,1,2,3,0:T(8,128)(2,1)S(1)}, bf16[1,32,8,2,128]{4,1,2,3,0:T(8,128)(2,1)S(1)}, u32[]{:S(2)}, u32[]{:S(2)}) collective-permute-start(bf16[1,32,8,2,128]{4,1,2,3,0:T(8,128)(2,1)S(1)} %collective-permute-done.3), channel_id=1, source_target_pairs={{0,28},{4,0},{8,4},{12,8},{16,12},{20,16},{24,20},{28,24},{1,29},{... | collective-permute-start | bytes 393224 | tf_op jit(solution)/shard_map/ppermute | solution.py:23
  51.7 2.8 %collective-permute-done.4 = bf16[1,32,8,2,128]{4,1,2,3,0:T(8,128)(2,1)S(1)} collective-permute-done((bf16[1,32,8,2,128]{4,1,2,3,0:T(8,128)(2,1)S(1)}, bf16[1,32,8,2,128]{4,1,2,3,0:T(8,128)(2,1)S(1)}, u32[]{:S(2)}, u32[]{:S(2)}) %collective-permute-start.4) | collective-permute-done | bytes 131104 | tf_op jit(solution)/shard_map/ppermute | solution.py:18
  54.5 6.1 %collective-permute-done.6 = bf16[1,32,8,2,128]{4,1,2,3,0:T(8,128)(2,1)S(1)} collective-permute-done((bf16[1,32,8,2,128]{4,1,2,3,0:T(8,128)(2,1)S(1)}, bf16[1,32,8,2,128]{4,1,2,3,0:T(8,128)(2,1)S(1)}, u32[]{:S(2)}, u32[]{:S(2)}) %collective-permute-start.6) | collective-permute-done | bytes 131104 | tf_op jit(solution)/shard_map/ppermute | solution.py:18
  63.7 2.0 %fusion.11 = bf16[64,128,16]{1,2,0:T(8,128)(2,1)} fusion(f32[64,128,16]{1,2,0:T(8,128)} %fusion.28, bf16[32,64,2,128]{3,0,1,2:T(8,128)(2,1)S(1)} %bitcast_dynamic-update-slice_fusion, s32[32]{0:T(128)S(1)} %bitcast.308, bf16[32]{0:T(256)(128)(2,1)S(1)} %get-tuple-element.5), kind=kOutput, calls=%fused_computation.23 | convolution fusion | flops 8651776 | bytes 1311744 | tf_op jit(solution)/shard_map/aqk,qsw->askw/dot_general | solution.py:48
  65.7 1.7 %squeeze.114 = bf16[64,2,1024]{2,1,0:T(2,128)(2,1)} reshape(bf16[1,64,16,128]{3,2,1,0:T(8,128)(2,1)} %bitcast.266) | data formatting | bytes 524288 | tf_op jit(solution)/shard_map/squeeze | solution.py:82
  67.4 1.8 %squeeze.119 = bf16[64,4,512]{2,1,0:T(4,128)(2,1)} reshape(bf16[1,64,16,128]{3,2,1,0:T(8,128)(2,1)} %bitcast.267) | data formatting | bytes 524288 | tf_op jit(solution)/shard_map/squeeze | solution.py:82
  70.3 1.2 fusion.52
  75.6 1.9 %fusion.80 = f32[4,64,512]{2,1,0:T(8,128)} fusion(bf16[32,4,512]{2,1,0:T(4,128)(2,1)S(1)} %copy-done.11, bf16[64,2,4,32]{0,3,2,1:T(8,128)(2,1)} %bitcast.292), kind=kOutput, calls=%fused_computation.124 | convolution fusion | flops 8388608 | bytes 688128 | tf_op jit(solution)/shard_map/rgm,sgr->sgm/dot_general | solution.py:33
  78.6 1.2 fusion.13
  86.3 8.9 %all_gather.3 = bf16[1,4,64,2,32]{2,4,3,0,1:T(8,128)(2,1)S(1)} all-gather(bf16[1,1,64,2,32]{2,4,3,0,1:T(8,128)(2,1)S(1)} %maximum_bitcast_fusion), channel_id=1, replica_groups=mesh['ang'=8,'row'=4] {'row'}, dimensions={1}, use_global_device_ids=true | all-gather | bytes 40960 | tf_op jit(solution)/shard_map/all_gather | solution.py:140
  98.1 1.2 fusion.19
  99.9 1.2 fusion.88
  101.1 1.2 fusion.90
  108.5 1.6 %subtract_bitcast_fusion = (f32[64,1,2048]{2,0,1:T(8,128)S(1)}, f32[64,1,2048]{2,0,1:T(8,128)S(1)}) fusion(f32[64,2048]{1,0:T(8,128)S(1)} %fusion, f32[]{:T(128)} %bitcast.69, f32[]{:T(128)} %bitcast, f32[64,2048]{1,0:T(8,128)S(1)} %fusion.64, bf16[64,32]{0,1:T(8,128)(2,1)S(1)} %fusion.23, bf16[1,2,32,2048]{3,2,1,0:T(8,128)(2,1)S(1)} %copy-done.2, ...), kind=kOutput, calls=%fused_computation.56 | convolution fusion | flops 9830400 | bytes 4333576 | tf_op jit(solution)/shard_map/rm,sr->sm/dot_general | solution.py:33
  111.2 29.8 %reduce-scatter.2.cloned.1.call-done = f32[8,2,2048]{2,0,1:T(8,128)} async-done(((f32[64,2,2048]{2,0,1:T(8,128)}), f32[8,2,2048]{2,0,1:T(8,128)}) %reduce-scatter.2.cloned.1.call-update) | async-done | bytes 131088 | tf_op jit(solution)/shard_map/reduce_scatter | solution.py:170
  141.0 1.7 %copy.146 = f32[8,2,2048]{2,1,0:T(2,128)} copy(f32[8,2,2048]{2,0,1:T(8,128)} %reduce-scatter.2.cloned.1.call-done) | data formatting | bytes 262144 | tf_op jit(solution)/shard_map/reduce_scatter | solution.py:170
  (160 shorter events, 36.8 us)
Async XLA Ops:
  6.5 6.2 %copy-start = (f32[8,2]{0,1:T(2,128)S(1)}, f32[8,2]{0,1:T(2,128)}, u32[]{:S(2)}) copy-start(f32[8,2]{0,1:T(2,128)} %param.15) | copy-start | bytes 196
  6.5 10.8 %copy-start.14 = (bf16[1,3,2,32,2048]{4,3,2,1,0:T(8,128)(2,1)S(1)}, bf16[1,3,2,32,2048]{4,3,2,1,0:T(8,128)(2,1)}, u32[]{:S(2)}) copy-start(bf16[1,3,2,32,2048]{4,3,2,1,0:T(8,128)(2,1)} %param.17) | copy-start | bytes 2359300
  6.5 134.4 %reduce-scatter.2.cloned.1.call-start = ((), (), s32[]{:S(2)}) async-start(), calls=%async_computation.1 | async-start | bytes 1179648 | tf_op jit(solution)/shard_map/reduce_scatter | solution.py:170
  8.2 32.5 %collective-permute-start = (bf16[1,32,8,2,128]{4,1,2,3,0:T(8,128)(2,1)}, bf16[1,32,8,2,128]{4,1,2,3,0:T(8,128)(2,1)}, u32[]{:S(2)}, u32[]{:S(2)}) collective-permute-start(bf16[1,32,8,2,128]{4,1,2,3,0:T(8,128)(2,1)} %copy.91), channel_id=1, source_target_pairs={{0,4},{4,8},{8,12},{12,16},{16,20},{20,24},{24,28},{28,0},{1,5},{5... | collective-permute-start | bytes 393224 | tf_op jit(solution)/shard_map/ppermute | solution.py:18
  8.7 32.1 %collective-permute-start.1 = (bf16[1,32,8,2,128]{4,1,2,3,0:T(8,128)(2,1)}, bf16[1,32,8,2,128]{4,1,2,3,0:T(8,128)(2,1)}, u32[]{:S(2)}, u32[]{:S(2)}) collective-permute-start(bf16[1,32,8,2,128]{4,1,2,3,0:T(8,128)(2,1)} %copy.91), channel_id=1, source_target_pairs={{0,28},{4,0},{8,4},{12,8},{16,12},{20,16},{24,20},{28,24},{1,29},{... | collective-permute-start | bytes 393224 | tf_op jit(solution)/shard_map/ppermute | solution.py:23
  12.7 5.6 %copy-start.4 = (bf16[1,2,2048,256]{3,2,1,0:T(8,128)(2,1)S(1)}, bf16[1,2,2048,256]{3,2,1,0:T(8,128)(2,1)}, u32[]{:S(2)}) copy-start(bf16[1,2,2048,256]{3,2,1,0:T(8,128)(2,1)} %param.16) | copy-start | bytes 6291460
  28.3 32.3 %copy-start.33 = (s32[1,32]{1,0:T(1,128)S(1)}, s32[1,32]{1,0:T(1,128)}, u32[]{:S(2)}) copy-start(s32[1,32]{1,0:T(1,128)} %param.13) | copy-start | bytes 388
  40.8 7.0 %collective-permute-start.2 = (bf16[1,32,8,2,128]{4,1,2,3,0:T(8,128)(2,1)}, bf16[1,32,8,2,128]{4,1,2,3,0:T(8,128)(2,1)S(1)}, u32[]{:S(2)}, u32[]{:S(2)}) collective-permute-start(bf16[1,32,8,2,128]{4,1,2,3,0:T(8,128)(2,1)} %collective-permute-done), channel_id=1, source_target_pairs={{0,4},{4,8},{8,12},{12,16},{16,20},{20,24},{24,28},{28,0},{1,5},{5... | collective-permute-start | bytes 393224 | tf_op jit(solution)/shard_map/ppermute | solution.py:18
  40.8 7.3 %collective-permute-start.3 = (bf16[1,32,8,2,128]{4,1,2,3,0:T(8,128)(2,1)}, bf16[1,32,8,2,128]{4,1,2,3,0:T(8,128)(2,1)S(1)}, u32[]{:S(2)}, u32[]{:S(2)}) collective-permute-start(bf16[1,32,8,2,128]{4,1,2,3,0:T(8,128)(2,1)} %collective-permute-done.1), channel_id=1, source_target_pairs={{0,28},{4,0},{8,4},{12,8},{16,12},{20,16},{24,20},{28,24},{1,29},{... | collective-permute-start | bytes 393224 | tf_op jit(solution)/shard_map/ppermute | solution.py:23
  47.8 6.7 %collective-permute-start.4 = (bf16[1,32,8,2,128]{4,1,2,3,0:T(8,128)(2,1)S(1)}, bf16[1,32,8,2,128]{4,1,2,3,0:T(8,128)(2,1)S(1)}, u32[]{:S(2)}, u32[]{:S(2)}) collective-permute-start(bf16[1,32,8,2,128]{4,1,2,3,0:T(8,128)(2,1)S(1)} %collective-permute-done.2), channel_id=1, source_target_pairs={{0,4},{4,8},{8,12},{12,16},{16,20},{20,24},{24,28},{28,0},{1,5},{5... | collective-permute-start | bytes 393224 | tf_op jit(solution)/shard_map/ppermute | solution.py:18
  48.0 6.5 %collective-permute-start.5 = (bf16[1,32,8,2,128]{4,1,2,3,0:T(8,128)(2,1)S(1)}, bf16[1,32,8,2,128]{4,1,2,3,0:T(8,128)(2,1)S(1)}, u32[]{:S(2)}, u32[]{:S(2)}) collective-permute-start(bf16[1,32,8,2,128]{4,1,2,3,0:T(8,128)(2,1)S(1)} %collective-permute-done.3), channel_id=1, source_target_pairs={{0,28},{4,0},{8,4},{12,8},{16,12},{20,16},{24,20},{28,24},{1,29},{... | collective-permute-start | bytes 393224 | tf_op jit(solution)/shard_map/ppermute | solution.py:23
  54.4 6.2 %collective-permute-start.6 = (bf16[1,32,8,2,128]{4,1,2,3,0:T(8,128)(2,1)S(1)}, bf16[1,32,8,2,128]{4,1,2,3,0:T(8,128)(2,1)S(1)}, u32[]{:S(2)}, u32[]{:S(2)}) collective-permute-start(bf16[1,32,8,2,128]{4,1,2,3,0:T(8,128)(2,1)S(1)} %collective-permute-done.4), channel_id=1, source_target_pairs={{0,4},{4,8},{8,12},{12,16},{16,20},{20,24},{24,28},{28,0},{1,5},{5... | collective-permute-start | bytes 393224 | tf_op jit(solution)/shard_map/ppermute | solution.py:18
  65.7 5.9 %copy-start.29 = (bf16[4,8,8,256]{3,2,1,0:T(8,128)(2,1)S(1)}, bf16[4,8,8,256]{3,2,1,0:T(8,128)(2,1)}, u32[]{:S(2)}) copy-start(bf16[4,8,8,256]{3,2,1,0:T(8,128)(2,1)} %copy.157) | copy-start | bytes 393220
  70.3 3.4 %copy-start.21 = (bf16[64,4,512]{2,1,0:T(4,128)(2,1)S(1)}, bf16[64,4,512]{2,1,0:T(4,128)(2,1)}, u32[]{:S(2)}) copy-start(bf16[64,4,512]{2,1,0:T(4,128)(2,1)} %squeeze.118) | copy-start | bytes 786436
  70.3 3.4 %copy-start.28 = (bf16[32,4,512]{2,1,0:T(4,128)(2,1)S(1)}, bf16[32,4,512]{2,1,0:T(4,128)(2,1)}, u32[]{:S(2)}) copy-start(bf16[32,4,512]{2,1,0:T(4,128)(2,1)} %reshape_squeeze.55) | copy-start | bytes 393220
  71.6 2.4 %copy-start.22 = (bf16[64,4,512]{2,1,0:T(4,128)(2,1)S(1)}, bf16[64,4,512]{2,1,0:T(4,128)(2,1)}, u32[]{:S(2)}) copy-start(bf16[64,4,512]{2,1,0:T(4,128)(2,1)} %squeeze.119) | copy-start | bytes 786436
  71.6 2.6 %copy-start.27 = (bf16[32,4,512]{2,1,0:T(4,128)(2,1)S(1)}, bf16[32,4,512]{2,1,0:T(4,128)(2,1)}, u32[]{:S(2)}) copy-start(bf16[32,4,512]{2,1,0:T(4,128)(2,1)} %reshape_squeeze.56) | copy-start | bytes 393220
  73.7 1.5 %copy-start.11 = (bf16[32,4,512]{2,1,0:T(4,128)(2,1)S(1)}, bf16[32,4,512]{2,1,0:T(4,128)(2,1)}, u32[]{:S(2)}) copy-start(bf16[32,4,512]{2,1,0:T(4,128)(2,1)} %reshape_squeeze.57) | copy-start | bytes 393220
  74.4 7.1 %copy-start.10 = (bf16[4,8,8,256]{3,2,1,0:T(8,128)(2,1)S(1)}, bf16[4,8,8,256]{3,2,1,0:T(8,128)(2,1)}, u32[]{:S(2)}) copy-start(bf16[4,8,8,256]{3,2,1,0:T(8,128)(2,1)} %copy.159) | copy-start | bytes 393220
  75.5 9.2 %copy-start.1 = (bf16[64,128,16]{1,2,0:T(8,128)(2,1)S(1)}, bf16[64,128,16]{1,2,0:T(8,128)(2,1)}, u32[]{:S(2)}) copy-start(bf16[64,128,16]{1,2,0:T(8,128)(2,1)} %fusion.11) | copy-start | bytes 786436
  79.8 15.4 %copy-start.34 = (bf16[4]{0:T(256)(128)(2,1)S(1)}, bf16[4]{0:T(256)(128)(2,1)}, u32[]{:S(2)}) copy-start(bf16[4]{0:T(256)(128)(2,1)} %compare_convert_fusion) | copy-start | bytes 28
  81.4 15.7 %copy-start.12 = (bf16[64,2,4,2,32]{0,4,3,2,1:T(8,128)(2,1)}, bf16[64,2,4,2,32]{0,4,3,2,1:T(8,128)(2,1)S(1)}, u32[]{:S(2)}) copy-start(bf16[64,2,4,2,32]{0,4,3,2,1:T(8,128)(2,1)S(1)} %rev.8) | copy-start | bytes 196612
  81.4 4.5 %copy-start.23 = (bf16[1,2,32,2048]{3,2,1,0:T(8,128)(2,1)S(1)}, bf16[1,2,32,2048]{3,2,1,0:T(8,128)(2,1)}, u32[]{:S(2)}) copy-start(bf16[1,2,32,2048]{3,2,1,0:T(8,128)(2,1)} %get-tuple-element.30) | copy-start | bytes 786436
  81.4 13.9 %copy-start.17 = (bf16[1,1,32,4,32]{4,3,2,1,0:T(4,128)(2,1)S(1)}, bf16[1,1,32,4,32]{4,3,2,1,0:T(4,128)(2,1)}, u32[]{:S(2)}) copy-start(bf16[1,1,32,4,32]{4,3,2,1,0:T(4,128)(2,1)} %get-tuple-element.24) | copy-start | bytes 24580
  81.4 15.4 %copy-start.20 = (bf16[64,2,1024]{2,1,0:T(2,128)(2,1)S(1)}, bf16[64,2,1024]{2,1,0:T(2,128)(2,1)}, u32[]{:S(2)}) copy-start(bf16[64,2,1024]{2,1,0:T(2,128)(2,1)} %squeeze.114) | copy-start | bytes 786436
  81.5 15.4 %copy-start.26 = (bf16[32,2,1024]{2,1,0:T(2,128)(2,1)S(1)}, bf16[32,2,1024]{2,1,0:T(2,128)(2,1)}, u32[]{:S(2)}) copy-start(bf16[32,2,1024]{2,1,0:T(2,128)(2,1)} %reshape_squeeze.51) | copy-start | bytes 393220
  81.5 15.6 %copy-start.19 = (bf16[64,2,1024]{2,1,0:T(2,128)(2,1)S(1)}, bf16[64,2,1024]{2,1,0:T(2,128)(2,1)}, u32[]{:S(2)}) copy-start(bf16[64,2,1024]{2,1,0:T(2,128)(2,1)} %squeeze.112) | copy-start | bytes 786436
  82.6 14.7 %copy-start.25 = (bf16[32,2,1024]{2,1,0:T(2,128)(2,1)S(1)}, bf16[32,2,1024]{2,1,0:T(2,128)(2,1)}, u32[]{:S(2)}) copy-start(bf16[32,2,1024]{2,1,0:T(2,128)(2,1)} %reshape_squeeze.52) | copy-start | bytes 393220
  86.3 16.0 %copy-start.8 = (bf16[32,2,1024]{2,1,0:T(2,128)(2,1)S(1)}, bf16[32,2,1024]{2,1,0:T(2,128)(2,1)}, u32[]{:S(2)}) copy-start(bf16[32,2,1024]{2,1,0:T(2,128)(2,1)} %reshape_squeeze.54) | copy-start | bytes 393220
  97.5 5.9 %copy-start.16 = (bf16[64,2,2,2,32]{0,4,3,2,1:T(8,128)(2,1)S(1)}, bf16[64,2,2,2,32]{0,4,3,2,1:T(8,128)(2,1)}, u32[]{:S(2)}) copy-start(bf16[64,2,2,2,32]{0,4,3,2,1:T(8,128)(2,1)} %copy-done.15) | copy-start | bytes 98308
  102.3 1.5 copy-start.5
  106.5 1.3 copy-start.2
  (11 other events, 10.4 us)
Sparse Core Ops, SparseCore 0:
  111.3 29.6 reduce-scatter.1
